TPU v7x, 128 devices: a whole 4x4x4 slice. The times are simulated.
128 devices in a mesh: section: 4 (over x), sample: 8 (over z, y_lo), tensor: 4 (over y_hi, core).
Axes of the slice: x: 4, y: 4 (y_hi: 2, y_lo: 2; y = y_hi * 2 + y_lo), z: 4, core: 2. Of those that a mesh axis runs over, the one named last changes fastest.
Arguments:
- queries: bfloat16 [4, 1024, 8192], P('section', 'sample', 'tensor'), may hold values from -4.5 to 4.5
- suffix_keys: bfloat16 [4, 1024, 1024], P('section', 'sample', 'tensor'), may hold values from -4.5 to 4.5
- suffix_values: bfloat16 [4, 1024, 1024], P('section', 'sample', 'tensor'), may hold values from -4.5 to 4.5
- output_grad: bfloat16 [4, 1024, 8192], P('section', 'sample', 'tensor'), may hold values from -192 to 192
- prefix_keys: bfloat16 [4, 4096, 1024], P('section', ('sample', 'tensor')), may hold values from -4.5 to 4.5
- prefix_values: bfloat16 [4, 4096, 1024], P('section', ('sample', 'tensor')), may hold values from -4.5 to 4.5
- kv_weight: bfloat16 [4, 8192, 2, 1024], P('section', None, None, 'tensor'), may hold values from -0.0625 to 0.0625
- prefix_states: bfloat16 [4, 4096, 8192], P('section', ('sample', 'tensor')), may hold values from -6 to 6
- norm_gain: bfloat16 [4, 8192], P('section'), may hold values from 0.099609375 to 1.8984375
- segment_ids: int32 [8, 128], P('sample'), may hold values from 0 to 1, never falling along the last dimension, each value on 1 to 96 neighbouring positions
- segment_prompt: int32 [8, 2], P('sample'), may hold values from 0 to 2
- block_table: int32 [3, 16], replicated, may hold values from 0 to 31, as said below
Outputs:
- query_grad: bfloat16 [4, 1024, 8192], P('section', 'sample', 'tensor')
- rollout_key_gradient: bfloat16 [4, 1024, 1024], P('section', 'sample', 'tensor')
- suffix_value_grad: bfloat16 [4, 1024, 1024], P('section', 'sample', 'tensor')
- prefix_key_grad: float32 [4, 4096, 1024], P('section', ('sample', 'tensor'))
- prefix_value_grad: float32 [4, 4096, 1024], P('section', ('sample', 'tensor'))
- prefix_state_gradient: float32 [4, 4096, 8192], P('section', ('sample', 'tensor'))
Inputs may be any that keep to these rules, and one draw needn't show every extreme that they name: `block_table`: each row lists 16 distinct pages; its first 8 entries are the same pages in every row, and every page of the pool appears in some row.
All inputs are finite; a program needn't handle non-finite values.
Results may differ from a plain program's by a relative error of at most 0.024.
Values may be sent and summed in bfloat16 or wider, within the bound.
No kernel may reach another device: no remote copies, remote signals or barrier semaphores. Data moves between devices by JAX's collectives and lax.ppermute only.
A program may use at most 192 MiB of HBM per device.

v0:
```python
import jax
import jax.numpy as jnp
from jax import lax
from jax.sharding import PartitionSpec as P

HEAD_SIZE = 128
PAGE = 128
MASKED_SCORE = -1e30
EPSILON = 1e-05


def visible_keys(seg_row, prompt_row, table, pooled_rows):
    tok_count = seg_row.shape[0]
    seg_hot = seg_row[:, None] == jnp.arange(prompt_row.shape[0], dtype=jnp.int32)[None, :]
    prompt_tok = jnp.sum(jnp.where(seg_hot, prompt_row[None, :], 0), axis=1)
    page_ids = jnp.arange(pooled_rows // PAGE, dtype=jnp.int32)
    member = jnp.any(table[:, :, None] == page_ids[None, None, :], axis=1)
    prompt_hot = prompt_tok[:, None] == jnp.arange(table.shape[0], dtype=jnp.int32)[None, :]
    member_tok = jnp.any(prompt_hot[:, :, None] & member[None, :, :], axis=1)
    prefix_seen = jnp.repeat(member_tok, PAGE, axis=1)
    position = jnp.arange(tok_count, dtype=jnp.int32)
    suffix_seen = (seg_row[:, None] == seg_row[None, :]) & (position[None, :] <= position[:, None])
    return jnp.concatenate([prefix_seen, suffix_seen], axis=1)


def attend_group(query_grp, grad_grp, key_rows, value_rows, visible):
    inv_root = query_grp.shape[-1] ** (-0.5)
    scores = (
        jnp.einsum("rgd,kd->rgk", query_grp, key_rows, preferred_element_type=jnp.float32)
        * inv_root
    )
    scores = jnp.where(visible[:, None, :], scores, MASKED_SCORE)
    row_max = jnp.max(scores, axis=2, keepdims=True)
    exponent = jnp.exp(scores - row_max)
    softmax_w = exponent / jnp.sum(exponent, axis=2, keepdims=True)
    weights_low = softmax_w.astype(jnp.bfloat16)
    attended = jnp.einsum(
        "rgk,kd->rgd", weights_low, value_rows, preferred_element_type=jnp.float32
    )
    delta_row = jnp.sum(grad_grp.astype(jnp.float32) * attended, axis=2, keepdims=True)
    weight_grad = jnp.einsum(
        "rgd,kd->rgk", grad_grp, value_rows, preferred_element_type=jnp.float32
    )
    score_grad = (softmax_w * (weight_grad - delta_row)).astype(jnp.bfloat16)
    query_out = (
        jnp.einsum("rgk,kd->rgd", score_grad, key_rows, preferred_element_type=jnp.float32)
        * inv_root
    )
    key_result = (
        jnp.einsum("rgk,rgd->kd", score_grad, query_grp, preferred_element_type=jnp.float32)
        * inv_root
    )
    value_out = jnp.einsum("rgk,rgd->kd", weights_low, grad_grp, preferred_element_type=jnp.float32)
    return (query_out, key_result, value_out)


def make_body(n_sec, n_smp, n_ten):

    def on_device(
        queries,
        suffix_keys,
        suffix_values,
        output_grad,
        prefix_keys,
        prefix_values,
        kv_weight,
        prefix_states,
        norm_gain,
        segment_ids,
        segment_prompt,
        block_table,
    ):
        head_width = suffix_keys.shape[2]
        kv_local = head_width // HEAD_SIZE
        rows_local = prefix_keys.shape[1]
        pooled_rows = rows_local * n_smp * n_ten
        block_rows = rows_local * n_ten
        tok_count = queries.shape[1]
        group_size = queries.shape[2] // head_width
        visible = visible_keys(segment_ids[0], segment_prompt[0], block_table, pooled_rows)
        query_rows = queries[0].reshape(tok_count, kv_local, group_size, HEAD_SIZE)
        grad_rows = output_grad[0].reshape(tok_count, kv_local, group_size, HEAD_SIZE)
        own_keys = suffix_keys[0]
        own_values = suffix_values[0]
        pk = prefix_keys[0].reshape(rows_local, n_ten, kv_local, HEAD_SIZE)
        pv = prefix_values[0].reshape(rows_local, n_ten, kv_local, HEAD_SIZE)
        query_pieces, suffix_key_pieces, suffix_value_pieces, reduced_pieces = ([], [], [], [])
        for head_index in range(kv_local):
            low_col = head_index * HEAD_SIZE
            send = jnp.concatenate([pk[:, :, head_index], pv[:, :, head_index]], axis=-1)
            send = send.transpose(1, 0, 2)
            got = lax.all_to_all(send, "tensor", 0, 0, tiled=True)
            got = got.reshape(block_rows, 2 * HEAD_SIZE)
            pool = lax.all_gather(got, "sample", axis=0, tiled=True)
            key_rows = jnp.concatenate(
                [pool[:, :HEAD_SIZE], own_keys[:, low_col : low_col + HEAD_SIZE]], axis=0
            )
            value_rows = jnp.concatenate(
                [pool[:, HEAD_SIZE:], own_values[:, low_col : low_col + HEAD_SIZE]], axis=0
            )
            query_out, key_result, value_out = attend_group(
                query_rows[:, head_index], grad_rows[:, head_index], key_rows, value_rows, visible
            )
            query_pieces.append(query_out)
            suffix_key_pieces.append(key_result[pooled_rows:])
            suffix_value_pieces.append(value_out[pooled_rows:])
            pool_grad = jnp.concatenate(
                [key_result[:pooled_rows], value_out[:pooled_rows]], axis=1
            ).astype(jnp.bfloat16)
            reduced_pieces.append(
                lax.psum_scatter(pool_grad, "sample", scatter_dimension=0, tiled=True)
            )
        query_grad = jnp.stack(query_pieces, axis=1).reshape(tok_count, -1).astype(jnp.bfloat16)
        rollout_key_gradient = jnp.concatenate(suffix_key_pieces, axis=1).astype(jnp.bfloat16)
        suffix_value_grad = jnp.concatenate(suffix_value_pieces, axis=1).astype(jnp.bfloat16)
        reduced = jnp.concatenate(reduced_pieces, axis=1)
        home_send = reduced.reshape(n_ten, rows_local, kv_local * 2 * HEAD_SIZE)
        home = lax.all_to_all(home_send, "tensor", 0, 0, tiled=True)
        home = home.reshape(n_ten, rows_local, kv_local, 2, HEAD_SIZE).transpose(3, 1, 0, 2, 4)
        home = home.reshape(2, rows_local, n_ten * kv_local * HEAD_SIZE).astype(jnp.float32)
        key_home = home[0]
        value_home = home[1]
        grad_cols = reduced.reshape(block_rows, kv_local, 2, HEAD_SIZE).transpose(0, 2, 1, 3)
        grad_cols = grad_cols.reshape(block_rows, 2, kv_local * HEAD_SIZE)
        group_term = lax.dot_general(
            grad_cols,
            kv_weight[0],
            (((1, 2), (1, 2)), ((), ())),
            preferred_element_type=jnp.float32,
        ).astype(jnp.bfloat16)
        width = group_term.shape[1]
        t_idx = lax.axis_index("tensor")
        core = t_idx % 2
        hi = t_idx // 2
        term4 = group_term.reshape(2, 2, rows_local, width)
        keep = lax.dynamic_index_in_dim(term4, core, 1, False)
        give = lax.dynamic_index_in_dim(term4, 1 - core, 1, False)
        core_pairs = [(i, i ^ 1) for i in range(n_ten)]
        got1 = lax.ppermute(give, "tensor", core_pairs)
        partial = keep.astype(jnp.float32) + got1.astype(jnp.float32)
        mine = lax.dynamic_index_in_dim(partial, hi, 0, False)
        other = lax.dynamic_index_in_dim(partial, 1 - hi, 0, False)
        chip_pairs = [(i, i ^ 2) for i in range(n_ten)]
        got2 = lax.ppermute(other.astype(jnp.bfloat16), "tensor", chip_pairs)
        normed_grad = mine + got2.astype(jnp.float32)
        states = prefix_states[0].astype(jnp.float32)
        gain_wide = norm_gain[0].astype(jnp.float32)[None, :]
        inv_rms = lax.rsqrt(jnp.mean(states * states, axis=1, keepdims=True) + EPSILON)
        gained = gain_wide * normed_grad
        layer_term = inv_rms * gained - states * inv_rms**3 * jnp.mean(
            states * gained, axis=1, keepdims=True
        )
        term_low = layer_term.astype(jnp.bfloat16)
        prefix_state_gradient = layer_term
        for shift in range(1, n_sec):
            pairs = [(l + shift, l) for l in range(n_sec - shift)]
            prefix_state_gradient = prefix_state_gradient + lax.ppermute(
                term_low, "section", pairs
            ).astype(jnp.float32)
        return (
            query_grad[None],
            rollout_key_gradient[None],
            suffix_value_grad[None],
            key_home[None],
            value_home[None],
            prefix_state_gradient[None],
        )

    return on_device


def solution(mesh):
    placed = (
        P("section", "sample", "tensor"),
        P("section", "sample", "tensor"),
        P("section", "sample", "tensor"),
        P("section", "sample", "tensor"),
        P("section", ("sample", "tensor"), None),
        P("section", ("sample", "tensor"), None),
        P("section", None, None, "tensor"),
        P("section", ("sample", "tensor"), None),
        P("section", None),
        P("sample", None),
        P("sample", None),
        P(),
    )
    body = make_body(mesh.shape["section"], mesh.shape["sample"], mesh.shape["tensor"])
    return jax.shard_map(
        body,
        mesh=mesh,
        in_specs=placed,
        out_specs=(
            P("section", "sample", "tensor"),
            P("section", "sample", "tensor"),
            P("section", "sample", "tensor"),
            P("section", ("sample", "tensor"), None),
            P("section", ("sample", "tensor"), None),
            P("section", ("sample", "tensor"), None),
        ),
        check_vma=False,
    )
```

profile of v0, /device:TPU:3, one launch (start us, length us, event | category | flops | bytes accessed | tf_op | source)
XLA Modules:
  0.0 443.0 jit_solution(18335856734817122372)
XLA Ops:
  10.4 11.5 %all_to_all.15 = bf16[4,128,256]{2,1,0:T(8,128)(2,1)} all-to-all(bf16[4,128,256]{2,1,0:T(8,128)(2,1)S(1)} %maximum_bitcast_fusion.12), channel_id=1, replica_groups=mesh['section'=4,'sample'=8,'tensor'=4] {'tensor'}, dimensions={0} | all-to-all | bytes 524288 | tf_op jit(solution)/shard_map/all_to_all | solution.py:92
  34.5 39.4 %all-gather.3.cloned.1.call-done = bf16[4096,256]{1,0:T(8,128)(2,1)} async-done(((bf16[512,256]{1,0:T(8,128)(2,1)}), bf16[4096,256]{1,0:T(8,128)(2,1)}) %all-gather.3.cloned.1.call-update) | async-done | bytes 2097168 | tf_op jit(solution)/shard_map/all_gather | solution.py:94
  80.0 10.7 %fusion.68 = (f32[128,8]{0,1:T(8,128)S(1)}, f32[128,8,4224]{0,2,1:T(8,128)}) fusion(f32[4224,128,8]{1,0,2:T(8,128)S(1)} %fusion.34, pred[128,4224]{0,1:T(8,128)(4,1)S(1)} %pad_add_fusion), kind=kOutput, calls=%fused_computation.127 | output fusion | flops 17305728 | bytes 35147776 | tf_op jit(solution)/shard_map/sub | solution.py:34
  90.8 7.5 %fusion.13 = bf16[128,8,4224]{0,2,1:T(8,128)(2,1)S(1)} fusion(f32[128,8,4224]{0,2,1:T(8,128)} %get-tuple-element.53, f32[128,8]{0,1:T(8,128)S(1)} %get-tuple-element.52), kind=kLoop, calls=%fused_computation.23 | loop fusion | flops 8650752 | bytes 25956352 | tf_op jit(solution)/shard_map/convert_element_type | solution.py:36
  105.5 6.2 %fusion.3 = bf16[128,8,4224]{0,2,1:T(8,128)(2,1)} fusion(f32[128,8]{0,1:T(8,128)S(1)} %fusion.29, f32[128,8,4224]{0,2,1:T(8,128)S(1)} %bitcast.189, f32[128,8]{0,1:T(8,128)S(1)} %get-tuple-element.52, bf16[128,128]{1,0:T(8,128)(2,1)} %get-tuple-element.44, bf16[4096,128]{1,0:T(8,128)(2,1)} %get-tuple-element.32, bf16[128,2,8,128]{0,3,2,1:T(8,128)(2,1)S(1)} %bitcast.199), kind=kOutput, calls=%fused_computation.6 | convolution fusion | flops 1126760448 | bytes 27303936 | tf_op jit(solution)/shard_map/rgd,kd->rgk/dot_general | solution.py:41
  111.7 6.5 %fusion.17 = bf16[4224,128]{0,1:T(8,128)(2,1)S(1)} fusion(bf16[128,8,4224]{0,2,1:T(8,128)(2,1)} %fusion.3, bf16[128,2,8,128]{0,3,2,1:T(8,128)(2,1)S(1)} %bitcast.194), kind=kOutput, calls=%fused_computation.34 | convolution fusion | flops 1108377600 | bytes 9994240 | tf_op jit(solution)/shard_map/rgk,rgd->kd/dot_general | solution.py:50
  134.4 10.4 %fusion.67 = (f32[128,8]{0,1:T(8,128)S(1)}, f32[128,8,4224]{0,2,1:T(8,128)}) fusion(f32[4224,128,8]{1,0,2:T(8,128)S(1)} %fusion.33, pred[128,4224]{0,1:T(8,128)(4,1)S(1)} %pad_add_fusion), kind=kOutput, calls=%fused_computation.126 | output fusion | flops 17305728 | bytes 35147776 | tf_op jit(solution)/shard_map/sub | solution.py:34
  144.8 7.6 %fusion.14 = bf16[128,8,4224]{0,2,1:T(8,128)(2,1)S(1)} fusion(f32[128,8,4224]{0,2,1:T(8,128)} %get-tuple-element.51, f32[128,8]{0,1:T(8,128)S(1)} %get-tuple-element.50), kind=kLoop, calls=%fused_computation.24 | loop fusion | flops 8650752 | bytes 25956352 | tf_op jit(solution)/shard_map/convert_element_type | solution.py:36
  159.5 6.1 %fusion.2 = bf16[128,8,4224]{0,2,1:T(8,128)(2,1)} fusion(f32[128,8]{0,1:T(8,128)S(1)} %fusion.30, f32[128,8,4224]{0,2,1:T(8,128)S(1)} %bitcast.187, f32[128,8]{0,1:T(8,128)S(1)} %get-tuple-element.50, bf16[128,128]{1,0:T(8,128)(2,1)S(1)} %copy-done.28, bf16[4096,128]{1,0:T(8,128)(2,1)} %get-tuple-element.34, bf16[128,2,8,128]{0,3,2,1:T(8,128)(2,1)S(1)} %bitcast.201), kind=kOutput, calls=%fused_computation.3 | convolution fusion | flops 1126760448 | bytes 27303936 | tf_op jit(solution)/shard_map/rgd,kd->rgk/dot_general | solution.py:41
  165.6 6.5 %fusion.18 = bf16[4224,128]{0,1:T(8,128)(2,1)S(1)} fusion(bf16[128,8,4224]{0,2,1:T(8,128)(2,1)} %fusion.2, bf16[128,2,8,128]{0,3,2,1:T(8,128)(2,1)S(1)} %bitcast.196), kind=kOutput, calls=%fused_computation.35 | convolution fusion | flops 1108377600 | bytes 9994240 | tf_op jit(solution)/shard_map/rgk,rgd->kd/dot_general | solution.py:50
  178.9 4.7 %reduce-scatter.3.cloned.1.call-done = bf16[512,256]{0,1:T(8,128)(2,1)} async-done(((bf16[4096,256]{0,1:T(8,128)(2,1)}), bf16[512,256]{0,1:T(8,128)(2,1)}) %reduce-scatter.3.cloned.1.call-update) | async-done | bytes 262160 | tf_op jit(solution)/shard_map/reduce_scatter | solution.py:111
  184.5 53.1 %reduce-scatter.5.cloned.1.call-done = bf16[512,256]{0,1:T(8,128)(2,1)} async-done(((bf16[4096,256]{0,1:T(8,128)(2,1)}), bf16[512,256]{0,1:T(8,128)(2,1)}) %reduce-scatter.5.cloned.1.call-update) | async-done | bytes 262160 | tf_op jit(solution)/shard_map/reduce_scatter | solution.py:111
  239.4 10.3 %bitcast_convert_fusion = bf16[512,8192]{1,0:T(8,128)(2,1)} fusion(bf16[512,2,256]{2,0,1:T(8,128)(2,1)S(1)} %reshape.173, bf16[8192,2,256]{2,1,0:T(2,128)(2,1)} %bitcast.216), kind=kOutput, calls=%fused_computation.10 | convolution fusion | flops 4299161600 | bytes 17301504 | tf_op jit(solution)/shard_map/dot_general | solution.py:125
  249.8 4.6 %dynamic-slice_bitcast_fusion = bf16[2,128,8192]{2,1,0:T(8,128)(2,1)} fusion(bf16[2,2,128,8192]{3,2,1,0:T(8,128)(2,1)} %bitcast.190, s32[]{:T(128)S(6)} %select_n.41), kind=kLoop, calls=%fused_computation.46 | loop fusion | bytes 8388612 | tf_op jit(solution)/shard_map/jit(dynamic_index_in_dim)/squeeze | solution.py:137
  255.5 7.1 %collective-permute-done = bf16[2,128,8192]{2,1,0:T(8,128)(2,1)} collective-permute-done((bf16[2,128,8192]{2,1,0:T(8,128)(2,1)}, bf16[2,128,8192]{2,1,0:T(8,128)(2,1)}, u32[]{:S(2)}, u32[]{:S(2)}) %collective-permute-start) | collective-permute-done | bytes 4194336 | tf_op jit(solution)/shard_map/ppermute | solution.py:139
  262.6 4.9 %convert_add_fusion = f32[2,128,8192]{2,1,0:T(8,128)S(1)} fusion(bf16[2,128,8192]{2,1,0:T(8,128)(2,1)} %collective-permute-done, bf16[2,2,128,8192]{3,2,1,0:T(8,128)(2,1)} %bitcast.191, s32[]{:T(128)S(6)} %select_n.40), kind=kLoop, calls=%fused_computation.21 | loop fusion | flops 6291456 | bytes 16777220 | tf_op jit(solution)/shard_map/add | solution.py:140
  275.0 5.0 %fusion.32 = bf16[128,1,8,128]{0,3,2,1:T(8,128)(2,1)S(1)} fusion(bf16[128,8,4224]{0,2,1:T(8,128)(2,1)} %fusion.3, bf16[128,128]{1,0:T(8,128)(2,1)S(1)} %copy-done.25, bf16[4096,128]{1,0:T(8,128)(2,1)S(1)} %copy-done.8), kind=kOutput, calls=%fused_computation.60 | convolution fusion | flops 1109721088 | bytes 9994240 | tf_op jit(solution)/shard_map/rgk,kd->rgd/dot_general | solution.py:46
  280.0 41.1 %collective-permute-done.1 = bf16[128,8192]{1,0:T(8,128)(2,1)} collective-permute-done((bf16[128,8192]{1,0:T(8,128)(2,1)}, bf16[128,8192]{1,0:T(8,128)(2,1)}, u32[]{:S(2)}, u32[]{:S(2)}) %collective-permute-start.1) | collective-permute-done | bytes 2097184 | tf_op jit(solution)/shard_map/ppermute | solution.py:144
  324.2 4.7 %fusion.58 = bf16[128,8192]{1,0:T(8,128)(2,1)} fusion(f32[128]{0:T(128)S(1)} %broadcast_multiply_fusion, f32[128]{0:T(128)S(1)} %get-tuple-element.49, bf16[1,128,8192]{2,1,0:T(8,128)(2,1)S(1)} %copy-done.2, bf16[128,8192]{1,0:T(8,128)(2,1)} %collective-permute-done.1, f32[2,128,8192]{2,1,0:T(8,128)S(1)} %copy-done.1, s32[]{:T(128)S(6)} %select_n.43, ...), kind=kLoop, calls=%fused_computation.117 | loop fusion | flops 9437184 | bytes 10520068 | tf_op jit(solution)/shard_map/convert_element_type | solution.py:153
  339.0 5.4 %all-to-all-start.2 = ((bf16[4,128,512]{1,2,0:T(8,128)(2,1)}), bf16[4,128,512]{1,2,0:T(8,128)(2,1)S(1)}, u32[]{:S(2)}, u32[]{:S(2)}) async-start(bf16[4,128,512]{1,2,0:T(8,128)(2,1)} %copy_bitcast_fusion), calls=%async_computation.4 | async-start | bytes 1048576 | tf_op jit(solution)/shard_map/all_to_all | solution.py:118
  347.7 6.0 %all-to-all-done.2 = bf16[4,128,512]{1,2,0:T(8,128)(2,1)S(1)} async-done(((bf16[4,128,512]{1,2,0:T(8,128)(2,1)}), bf16[4,128,512]{1,2,0:T(8,128)(2,1)S(1)}, u32[]{:S(2)}, u32[]{:S(2)}) %all-to-all-start.2) | async-done | bytes 524320 | tf_op jit(solution)/shard_map/all_to_all | solution.py:118
  355.9 24.9 %collective-permute-done.3 = bf16[128,8192]{1,0:T(8,128)(2,1)} collective-permute-done((bf16[128,8192]{1,0:T(8,128)(2,1)}, bf16[128,8192]{1,0:T(8,128)(2,1)}, u32[]{:S(2)}, u32[]{:S(2)}) %collective-permute-start.3) | collective-permute-done | bytes 2097184 | tf_op jit(solution)/shard_map/ppermute | solution.py:157
  380.8 46.5 %collective-permute-done.2 = bf16[128,8192]{1,0:T(8,128)(2,1)} collective-permute-done((bf16[128,8192]{1,0:T(8,128)(2,1)}, bf16[128,8192]{1,0:T(8,128)(2,1)}, u32[]{:S(2)}, u32[]{:S(2)}) %collective-permute-start.2) | collective-permute-done | bytes 2097184 | tf_op jit(solution)/shard_map/ppermute | solution.py:157
  427.2 9.0 %add_bitcast_fusion = f32[1,128,8192]{2,1,0:T(8,128)} fusion(bf16[128,8192]{1,0:T(8,128)(2,1)} %collective-permute-done.4, bf16[128,8192]{1,0:T(8,128)(2,1)} %collective-permute-done.3, bf16[128,8192]{1,0:T(8,128)(2,1)} %collective-permute-done.2, f32[128]{0:T(128)S(1)} %broadcast_multiply_fusion, f32[128]{0:T(128)S(1)} %get-tuple-element.49, ...), kind=kLoop, calls=%fused_computation.44 | loop fusion | flops 14680064 | bytes 18908676 | tf_op jit(solution)/shard_map/broadcast_in_dim | solution.py:166
  (173 shorter events, 88.2 us)
Async XLA Ops:
  7.2 20.0 %copy-start.20 = (bf16[1,128,2048]{2,1,0:T(8,128)(2,1)S(1)}, bf16[1,128,2048]{2,1,0:T(8,128)(2,1)}, u32[]{:S(2)}) copy-start(bf16[1,128,2048]{2,1,0:T(8,128)(2,1)} %param.12) | copy-start | bytes 1572868
  7.2 20.3 %copy-start.21 = (bf16[1,128,2048]{2,1,0:T(8,128)(2,1)S(1)}, bf16[1,128,2048]{2,1,0:T(8,128)(2,1)}, u32[]{:S(2)}) copy-start(bf16[1,128,2048]{2,1,0:T(8,128)(2,1)} %param.15) | copy-start | bytes 1572868
  7.2 66.8 %all-gather.3.cloned.1.call-start = ((), (), s32[]{:S(2)}) async-start(), calls=%async_computation.5 | async-start | bytes 2359296 | tf_op jit(solution)/shard_map/all_gather | solution.py:94
  10.3 18.5 %copy-start.30 = (s32[1,128]{1,0:T(1,128)S(1)}, s32[1,128]{1,0:T(1,128)}, u32[]{:S(2)}) copy-start(s32[1,128]{1,0:T(1,128)} %param.21) | copy-start | bytes 1540
  10.3 18.5 %copy-start.32 = (s32[1,2]{1,0:T(1,128)S(1)}, s32[1,2]{1,0:T(1,128)}, u32[]{:S(2)}) copy-start(s32[1,2]{1,0:T(1,128)} %param.22) | copy-start | bytes 28
  10.3 18.6 %copy-start.31 = (s32[3,16]{1,0:T(4,128)S(1)}, s32[3,16]{1,0:T(4,128)}, u32[]{:S(2)}) copy-start(s32[3,16]{1,0:T(4,128)} %param.23) | copy-start | bytes 580
  10.3 18.9 %copy-start.26 = (bf16[1,128,256]{2,1,0:T(8,128)(2,1)S(1)}, bf16[1,128,256]{2,1,0:T(8,128)(2,1)}, u32[]{:S(2)}) copy-start(bf16[1,128,256]{2,1,0:T(8,128)(2,1)} %param.13) | copy-start | bytes 196612
  22.8 11.0 %all-to-all-start.1 = ((bf16[4,128,256]{2,1,0:T(8,128)(2,1)}), bf16[4,128,256]{2,1,0:T(8,128)(2,1)S(1)}, u32[]{:S(2)}, u32[]{:S(2)}) async-start(bf16[4,128,256]{2,1,0:T(8,128)(2,1)} %maximum_bitcast_fusion.13), calls=%async_computation.1 | async-start | bytes 524288 | tf_op jit(solution)/shard_map/all_to_all | solution.py:92
  27.2 101.2 %all-gather.5.cloned.1.call-start = ((), (), s32[]{:S(2)}) async-start(), calls=%async_computation.6 | async-start | bytes 2359296 | tf_op jit(solution)/shard_map/all_gather | solution.py:94
  34.5 43.1 %copy-start.24 = (bf16[128,128]{1,0:T(8,128)(2,1)S(1)}, bf16[128,128]{1,0:T(8,128)(2,1)}, u32[]{:S(2)}) copy-start(bf16[128,128]{1,0:T(8,128)(2,1)} %get-tuple-element.46) | copy-start | bytes 98308
  34.5 149.1 %reduce-scatter.3.cloned.1.call-start = ((), (), s32[]{:S(2)}) async-start(), calls=%async_computation.7 | async-start | bytes 2359296 | tf_op jit(solution)/shard_map/reduce_scatter | solution.py:111
  90.8 14.5 %slice-start.6 = ((s8[17301504]{0:T(1024)(128)(4,1)}), s8[4194304]{0:T(1024)(128)(4,1)S(1)}, s32[]{:S(2)}) async-start(s8[17301504]{0:T(1024)(128)(4,1)} %bitcast.188), calls=%async_computation.15 | async-start | bytes 8388608
  90.8 14.5 %slice-start.7 = ((s8[17301504]{0:T(1024)(128)(4,1)}), s8[4194304]{0:T(1024)(128)(4,1)S(1)}, s32[]{:S(2)}) async-start(s8[17301504]{0:T(1024)(128)(4,1)} %bitcast.188), calls=%async_computation.16 | async-start | bytes 8388608
  90.8 14.5 %slice-start.8 = ((s8[17301504]{0:T(1024)(128)(4,1)}), s8[4194304]{0:T(1024)(128)(4,1)S(1)}, s32[]{:S(2)}) async-start(s8[17301504]{0:T(1024)(128)(4,1)} %bitcast.188), calls=%async_computation.17 | async-start | bytes 8388608
  123.8 113.9 %reduce-scatter.5.cloned.1.call-start = ((), (), s32[]{:S(2)}) async-start(), calls=%async_computation.8 | async-start | bytes 2359296 | tf_op jit(solution)/shard_map/reduce_scatter | solution.py:111
  144.8 14.5 %slice-start.2 = ((s8[17301504]{0:T(1024)(128)(4,1)}), s8[4194304]{0:T(1024)(128)(4,1)S(1)}, s32[]{:S(2)}) async-start(s8[17301504]{0:T(1024)(128)(4,1)} %bitcast.186), calls=%async_computation.11 | async-start | bytes 8388608
  254.4 8.2 %collective-permute-start = (bf16[2,128,8192]{2,1,0:T(8,128)(2,1)}, bf16[2,128,8192]{2,1,0:T(8,128)(2,1)}, u32[]{:S(2)}, u32[]{:S(2)}) collective-permute-start(bf16[2,128,8192]{2,1,0:T(8,128)(2,1)} %dynamic-slice_bitcast_fusion), channel_id=1, source_target_pairs={{0,1},{1,0},{2,3},{3,2},{4,5},{5,4},{6,7},{7,6},{8,9},{9,8},{10,11... | collective-permute-start | bytes 12582920 | tf_op jit(solution)/shard_map/ppermute | solution.py:139
  272.4 48.7 %collective-permute-start.1 = (bf16[128,8192]{1,0:T(8,128)(2,1)}, bf16[128,8192]{1,0:T(8,128)(2,1)}, u32[]{:S(2)}, u32[]{:S(2)}) collective-permute-start(bf16[128,8192]{1,0:T(8,128)(2,1)} %fusion.26), channel_id=1, source_target_pairs={{0,2},{1,3},{2,0},{3,1},{4,6},{5,7},{6,4},{7,5},{8,10},{9,11},{10,... | collective-permute-start | bytes 6291464 | tf_op jit(solution)/shard_map/ppermute | solution.py:144
  274.9 46.2 %copy-start.1 = (f32[2,128,8192]{2,1,0:T(8,128)S(1)}, f32[2,128,8192]{2,1,0:T(8,128)}, u32[]{:S(2)}) copy-start(f32[2,128,8192]{2,1,0:T(8,128)} %copy-done) | copy-start | bytes 25165828
  274.9 46.2 %copy-start.2 = (bf16[1,128,8192]{2,1,0:T(8,128)(2,1)S(1)}, bf16[1,128,8192]{2,1,0:T(8,128)(2,1)}, u32[]{:S(2)}) copy-start(bf16[1,128,8192]{2,1,0:T(8,128)(2,1)} %param.19) | copy-start | bytes 6291460
  328.9 27.0 %collective-permute-start.4 = (bf16[128,8192]{1,0:T(8,128)(2,1)}, bf16[128,8192]{1,0:T(8,128)(2,1)}, u32[]{:S(2)}, u32[]{:S(2)}) collective-permute-start(bf16[128,8192]{1,0:T(8,128)(2,1)} %fusion.58), channel_id=1, source_target_pairs={{96,0},{97,1},{98,2},{99,3},{100,4},{101,5},{102,6},{103,7},{104,8... | collective-permute-start | bytes 6291464 | tf_op jit(solution)/shard_map/ppermute | solution.py:157
  331.0 49.7 %collective-permute-start.3 = (bf16[128,8192]{1,0:T(8,128)(2,1)}, bf16[128,8192]{1,0:T(8,128)(2,1)}, u32[]{:S(2)}, u32[]{:S(2)}) collective-permute-start(bf16[128,8192]{1,0:T(8,128)(2,1)} %fusion.58), channel_id=1, source_target_pairs={{64,0},{96,32},{65,1},{97,33},{66,2},{98,34},{67,3},{99,35},{68,4}... | collective-permute-start | bytes 6291464 | tf_op jit(solution)/shard_map/ppermute | solution.py:157
  332.3 94.9 %collective-permute-start.2 = (bf16[128,8192]{1,0:T(8,128)(2,1)}, bf16[128,8192]{1,0:T(8,128)(2,1)}, u32[]{:S(2)}, u32[]{:S(2)}) collective-permute-start(bf16[128,8192]{1,0:T(8,128)(2,1)} %fusion.58), channel_id=1, source_target_pairs={{32,0},{64,32},{96,64},{33,1},{65,33},{97,65},{34,2},{66,34},{98,6... | collective-permute-start | bytes 6291464 | tf_op jit(solution)/shard_map/ppermute | solution.py:157
  339.0 14.8 %all-to-all-start.2 = ((bf16[4,128,512]{1,2,0:T(8,128)(2,1)}), bf16[4,128,512]{1,2,0:T(8,128)(2,1)S(1)}, u32[]{:S(2)}, u32[]{:S(2)}) async-start(bf16[4,128,512]{1,2,0:T(8,128)(2,1)} %copy_bitcast_fusion), calls=%async_computation.4 | async-start | bytes 1048576 | tf_op jit(solution)/shard_map/all_to_all | solution.py:118
  (33 other events, 245.7 us)
Sparse Core Ops, SparseCore 0:
  22.1 51.7 all-gather.2
  76.2 52.1 all-gather.4
  131.3 52.1 reduce-scatter.2
  185.8 51.8 reduce-scatter.4
where the time goes:
time: 448 us; the launch traced here: 443 us
  waiting for transfers between devices  230 us (51%)
  other arithmetic  62.3 us (14%)
  matrix products  57.7 us (13%)
  local copies, waits for them, and re-layouts  48.1 us (11%)
  starting transfers between devices  18.8 us (4%)
  between operations  14.8 us (3%)
  blocking collectives  11.5 us (3%)
    ppermute x3, waiting for transfers between devices, on_device(): lax.ppermute(term_low, 'section', pairs).astype(jnp.float32)  71.3 us
    reduce_scatter x2, waiting for transfers between devices, on_device(): lax.psum_scatter(pool_grad, 'sample', scatter_dimension=0, tiled=True)  57.8 us
    all_gather x2, waiting for transfers between devices, on_device(): pool = lax.all_gather(got, 'sample', axis=0, tiled=True)  44 us
    ppermute x1, waiting for transfers between devices, on_device(): got2 = lax.ppermute(other.astype(jnp.bfloat16), 'tensor', chip_pairs)  41.1 us
    unnamed x100, local copies, waits for them, and re-layouts  23.1 us
    sub x2, other arithmetic, attend_group(): exponent = jnp.exp(scores - row_max)  21.1 us
    convert_element_type x2, other arithmetic, attend_group(): weights_low = softmax_w.astype(jnp.bfloat16)  15.1 us
    dot_general x2, matrix products, attend_group(): jnp.einsum('rgk,rgd->kd', score_grad, query_grp, preferred_element_type=j...  13 us
  transfers between devices with their start and end apart: 11, of which 10 were waited for; matrix products, arithmetic and copies ran while one was open for 24% of the time, Pallas kernels for 0%

commit v1 on v0

--- a/solution.py
+++ b/solution.py
@@ -91,7 +91,9 @@
             send = send.transpose(1, 0, 2)
             got = lax.all_to_all(send, "tensor", 0, 0, tiled=True)
             got = got.reshape(block_rows, 2 * HEAD_SIZE)
-            pool = lax.all_gather(got, "sample", axis=0, tiled=True)
+            pool = jnp.concatenate(
+                lax.all_to_all(jnp.stack([got] * lax.axis_size("sample")), "sample", 0, 0), axis=0
+            )
             key_rows = jnp.concatenate(
                 [pool[:, :HEAD_SIZE], own_keys[:, low_col : low_col + HEAD_SIZE]], axis=0
             )

time: 448 us -> 463 us (1.033)
  starting transfers between devices: 18.8 us -> 33.5 us
  blocking collectives: 11.5 us -> 0 us
  waiting for transfers between devices: 230 us -> 236 us
  matrix products: 57.7 us -> 62.4 us
    all_gather x2 -> x0, waiting for transfers between devices: 44 us -> none  [on_device(): pool = lax.all_gather(got, 'sample', axis=0, tiled=True)]
    all_to_all x0 -> x2, waiting for transfers between devices: none -> 40.5 us  [on_device(): lax.all_to_all(jnp.stack([got] * lax.axis_size('sample')), 'sample', 0, 0)]
    all_to_all x1 -> x0, blocking collectives: 11.5 us -> none  [on_device(): got = lax.all_to_all(send, 'tensor', 0, 0, tiled=True)]
    all_to_all x1 -> x2, waiting for transfers between devices: 2.29 us -> 12.2 us  [on_device(): got = lax.all_to_all(send, 'tensor', 0, 0, tiled=True)]
    all_to_all x0 -> x2, starting transfers between devices: none -> 9.63 us  [on_device(): lax.all_to_all(jnp.stack([got] * lax.axis_size('sample')), 'sample', 0, 0)]
    all_to_all x1 -> x2, starting transfers between devices: 4.41 us -> 9.48 us  [on_device(): got = lax.all_to_all(send, 'tensor', 0, 0, tiled=True)]
  transfers between devices with their start and end apart: 11 -> 12, of which waited for: 10 -> 11; matrix products, arithmetic and copies ran while one was open for 24% -> 15% of each run, Pallas kernels for 0% -> 0%
where the time goes in v1:
time: 463 us; the launch traced here: 458 us
  waiting for transfers between devices  236 us (51%)
  other arithmetic  63.2 us (14%)
  matrix products  62.4 us (13%)
  local copies, waits for them, and re-layouts  47.4 us (10%)
  starting transfers between devices  33.5 us (7%)
  between operations  15 us (3%)
    ppermute x3, waiting for transfers between devices, on_device(): lax.ppermute(term_low, 'section', pairs).astype(jnp.float32)  72 us
    reduce_scatter x2, waiting for transfers between devices, on_device(): lax.psum_scatter(pool_grad, 'sample', scatter_dimension=0, tiled=True)  57.4 us
    ppermute x1, waiting for transfers between devices, on_device(): got2 = lax.ppermute(other.astype(jnp.bfloat16), 'tensor', chip_pairs)  40.9 us
    all_to_all x2, waiting for transfers between devices, on_device(): lax.all_to_all(jnp.stack([got] * lax.axis_size('sample')), 'sample', 0, 0)  40.5 us
    unnamed x100, local copies, waits for them, and re-layouts  23 us
    sub x2, other arithmetic, attend_group(): exponent = jnp.exp(scores - row_max)  21.1 us
    convert_element_type x2, other arithmetic, attend_group(): weights_low = softmax_w.astype(jnp.bfloat16)  14.3 us
    dot_general x2, matrix products, attend_group(): jnp.einsum('rgd,kd->rgk', grad_grp, value_rows, preferred_element_type=jn...  14.2 us
  transfers between devices with their start and end apart: 12, of which 11 were waited for; matrix products, arithmetic and copies ran while one was open for 15% of the time, Pallas kernels for 0%

profile of v1, /device:TPU:3, one launch (start us, length us, event | category | flops | bytes accessed | tf_op | source)
XLA Modules:
  0.0 457.6 jit_solution(6521664231095195686)
XLA Ops:
  10.2 5.1 %all-to-all-start.2 = ((bf16[4,128,256]{1,2,0:T(8,128)(2,1)}), bf16[4,128,256]{1,2,0:T(8,128)(2,1)S(1)}, u32[]{:S(2)}, u32[]{:S(2)}) async-start(bf16[4,128,256]{1,2,0:T(8,128)(2,1)} %maximum_bitcast_fusion.13), calls=%async_computation.2 | async-start | bytes 524288 | tf_op jit(solution)/shard_map/all_to_all | solution.py:92
  16.0 5.8 %all-to-all-done.2 = bf16[4,128,256]{1,2,0:T(8,128)(2,1)S(1)} async-done(((bf16[4,128,256]{1,2,0:T(8,128)(2,1)}), bf16[4,128,256]{1,2,0:T(8,128)(2,1)S(1)}, u32[]{:S(2)}, u32[]{:S(2)}) %all-to-all-start.2) | async-done | bytes 262176 | tf_op jit(solution)/shard_map/all_to_all | solution.py:92
  26.4 6.4 %all-to-all-done = bf16[4,128,256]{1,2,0:T(8,128)(2,1)S(1)} async-done(((bf16[4,128,256]{1,2,0:T(8,128)(2,1)}), bf16[4,128,256]{1,2,0:T(8,128)(2,1)S(1)}, u32[]{:S(2)}, u32[]{:S(2)}) %all-to-all-start) | async-done | bytes 262176 | tf_op jit(solution)/shard_map/all_to_all | solution.py:92
  34.2 5.1 %all-to-all-start.3 = ((bf16[8,512,256]{2,1,0:T(8,128)(2,1)}), bf16[8,512,256]{2,1,0:T(8,128)(2,1)S(1)}, u32[]{:S(2)}, u32[]{:S(2)}) async-start(bf16[8,512,256]{2,1,0:T(8,128)(2,1)} %stack.20), calls=%async_computation.3 | async-start | bytes 4194304 | tf_op jit(solution)/shard_map/all_to_all | solution.py:95
  43.0 22.2 %all-to-all-done.3 = bf16[8,512,256]{2,1,0:T(8,128)(2,1)S(1)} async-done(((bf16[8,512,256]{2,1,0:T(8,128)(2,1)}), bf16[8,512,256]{2,1,0:T(8,128)(2,1)S(1)}, u32[]{:S(2)}, u32[]{:S(2)}) %all-to-all-start.3) | async-done | bytes 2097184 | tf_op jit(solution)/shard_map/all_to_all | solution.py:95
  78.0 18.2 %all-to-all-done.1 = bf16[8,512,256]{2,1,0:T(8,128)(2,1)} async-done(((bf16[8,512,256]{2,1,0:T(8,128)(2,1)}), bf16[8,512,256]{2,1,0:T(8,128)(2,1)}, u32[]{:S(2)}, u32[]{:S(2)}) %all-to-all-start.1) | async-done | bytes 2097184 | tf_op jit(solution)/shard_map/all_to_all | solution.py:95
  103.2 10.7 %fusion.66 = (f32[128,8]{0,1:T(8,128)S(1)}, f32[128,8,4224]{0,2,1:T(8,128)}) fusion(f32[4224,128,8]{1,0,2:T(8,128)S(1)} %fusion.34, pred[128,4224]{0,1:T(8,128)(4,1)S(1)} %pad_add_fusion), kind=kOutput, calls=%fused_computation.125 | output fusion | flops 17305728 | bytes 35147776 | tf_op jit(solution)/shard_map/sub | solution.py:34
  114.0 6.8 %fusion.13 = bf16[128,8,4224]{0,2,1:T(8,128)(2,1)S(1)} fusion(f32[128,8,4224]{0,2,1:T(8,128)} %get-tuple-element.59, f32[128,8]{0,1:T(8,128)S(1)} %get-tuple-element.58), kind=kLoop, calls=%fused_computation.23 | loop fusion | flops 8650752 | bytes 25956352 | tf_op jit(solution)/shard_map/convert_element_type | solution.py:36
  127.5 7.1 %fusion.3 = bf16[128,8,4224]{0,2,1:T(8,128)(2,1)} fusion(f32[128,8]{0,1:T(8,128)S(1)} %fusion.29, f32[128,8,4224]{0,2,1:T(8,128)S(1)} %bitcast.191, f32[128,8]{0,1:T(8,128)S(1)} %get-tuple-element.58, bf16[128,128]{1,0:T(8,128)(2,1)S(1)} %get-tuple-element.50, bf16[4096,128]{1,0:T(8,128)(2,1)} %get-tuple-element.38, bf16[128,2,8,128]{0,3,2,1:T(8,128)(2,1)} %bitcast.204), kind=kOutput, calls=%fused_computation.6 | convolution fusion | flops 1126760448 | bytes 27303936 | tf_op jit(solution)/shard_map/rgd,kd->rgk/dot_general | solution.py:41
  134.6 6.4 %fusion.17 = bf16[4224,128]{0,1:T(8,128)(2,1)S(1)} fusion(bf16[128,8,4224]{0,2,1:T(8,128)(2,1)} %fusion.3, bf16[128,2,8,128]{0,3,2,1:T(8,128)(2,1)} %bitcast.199), kind=kOutput, calls=%fused_computation.34 | convolution fusion | flops 1108377600 | bytes 9994240 | tf_op jit(solution)/shard_map/rgk,rgd->kd/dot_general | solution.py:50
  148.2 10.4 %fusion.65 = (f32[128,8]{0,1:T(8,128)S(1)}, f32[128,8,4224]{0,2,1:T(8,128)}) fusion(f32[4224,128,8]{1,0,2:T(8,128)S(1)} %fusion.33, pred[128,4224]{0,1:T(8,128)(4,1)S(1)} %pad_add_fusion), kind=kOutput, calls=%fused_computation.124 | output fusion | flops 17305728 | bytes 35147776 | tf_op jit(solution)/shard_map/sub | solution.py:34
  158.7 7.6 %fusion.14 = bf16[128,8,4224]{0,2,1:T(8,128)(2,1)S(1)} fusion(f32[128,8,4224]{0,2,1:T(8,128)} %get-tuple-element.57, f32[128,8]{0,1:T(8,128)S(1)} %get-tuple-element.56), kind=kLoop, calls=%fused_computation.24 | loop fusion | flops 8650752 | bytes 25956352 | tf_op jit(solution)/shard_map/convert_element_type | solution.py:36
  173.4 7.1 %fusion.2 = bf16[128,8,4224]{0,2,1:T(8,128)(2,1)} fusion(f32[128,8]{0,1:T(8,128)S(1)} %fusion.30, f32[128,8,4224]{0,2,1:T(8,128)S(1)} %bitcast.193, f32[128,8]{0,1:T(8,128)S(1)} %get-tuple-element.56, bf16[128,128]{1,0:T(8,128)(2,1)S(1)} %get-tuple-element.51, bf16[4096,128]{1,0:T(8,128)(2,1)} %get-tuple-element.40, bf16[128,2,8,128]{0,3,2,1:T(8,128)(2,1)} %bitcast.205), kind=kOutput, calls=%fused_computation.3 | convolution fusion | flops 1126760448 | bytes 27303936 | tf_op jit(solution)/shard_map/rgd,kd->rgk/dot_general | solution.py:41
  180.5 6.5 %fusion.18 = bf16[4224,128]{0,1:T(8,128)(2,1)S(1)} fusion(bf16[128,8,4224]{0,2,1:T(8,128)(2,1)} %fusion.2, bf16[128,2,8,128]{0,3,2,1:T(8,128)(2,1)S(1)} %bitcast.201), kind=kOutput, calls=%fused_computation.35 | convolution fusion | flops 1108377600 | bytes 9994240 | tf_op jit(solution)/shard_map/rgk,rgd->kd/dot_general | solution.py:50
  198.8 53.3 %reduce-scatter.5.cloned.1.call-done = bf16[512,256]{0,1:T(8,128)(2,1)} async-done(((bf16[4096,256]{0,1:T(8,128)(2,1)}), bf16[512,256]{0,1:T(8,128)(2,1)}) %reduce-scatter.5.cloned.1.call-update) | async-done | bytes 262160 | tf_op jit(solution)/shard_map/reduce_scatter | solution.py:113
  254.0 10.1 %bitcast_convert_fusion = bf16[512,8192]{1,0:T(8,128)(2,1)} fusion(bf16[512,2,256]{2,0,1:T(8,128)(2,1)S(1)} %reshape.177, bf16[8192,2,256]{2,1,0:T(2,128)(2,1)} %bitcast.223), kind=kOutput, calls=%fused_computation.10 | convolution fusion | flops 4299161600 | bytes 17301504 | tf_op jit(solution)/shard_map/dot_general | solution.py:127
  269.9 7.1 %collective-permute-done = bf16[2,128,8192]{2,1,0:T(8,128)(2,1)} collective-permute-done((bf16[2,128,8192]{2,1,0:T(8,128)(2,1)}, bf16[2,128,8192]{2,1,0:T(8,128)(2,1)}, u32[]{:S(2)}, u32[]{:S(2)}) %collective-permute-start) | collective-permute-done | bytes 4194336 | tf_op jit(solution)/shard_map/ppermute | solution.py:141
  289.3 5.3 %fusion.32 = bf16[128,1,8,128]{0,3,2,1:T(8,128)(2,1)S(1)} fusion(bf16[128,8,4224]{0,2,1:T(8,128)(2,1)} %fusion.3, bf16[128,128]{1,0:T(8,128)(2,1)S(1)} %copy-done.23, bf16[4096,128]{1,0:T(8,128)(2,1)} %copy-done.6), kind=kOutput, calls=%fused_computation.60 | convolution fusion | flops 1109721088 | bytes 9994240 | tf_op jit(solution)/shard_map/rgk,kd->rgd/dot_general | solution.py:46
  294.6 40.9 %collective-permute-done.1 = bf16[128,8192]{1,0:T(8,128)(2,1)} collective-permute-done((bf16[128,8192]{1,0:T(8,128)(2,1)}, bf16[128,8192]{1,0:T(8,128)(2,1)}, u32[]{:S(2)}, u32[]{:S(2)}) %collective-permute-start.1) | collective-permute-done | bytes 2097184 | tf_op jit(solution)/shard_map/ppermute | solution.py:146
  352.6 5.4 %all-to-all-start.4 = ((bf16[4,128,512]{1,2,0:T(8,128)(2,1)}), bf16[4,128,512]{1,2,0:T(8,128)(2,1)S(1)}, u32[]{:S(2)}, u32[]{:S(2)}) async-start(bf16[4,128,512]{1,2,0:T(8,128)(2,1)} %copy_bitcast_fusion), calls=%async_computation.6 | async-start | bytes 1048576 | tf_op jit(solution)/shard_map/all_to_all | solution.py:120
  361.3 6.0 %all-to-all-done.4 = bf16[4,128,512]{1,2,0:T(8,128)(2,1)S(1)} async-done(((bf16[4,128,512]{1,2,0:T(8,128)(2,1)}), bf16[4,128,512]{1,2,0:T(8,128)(2,1)S(1)}, u32[]{:S(2)}, u32[]{:S(2)}) %all-to-all-start.4) | async-done | bytes 524320 | tf_op jit(solution)/shard_map/all_to_all | solution.py:120
  369.5 25.6 %collective-permute-done.3 = bf16[128,8192]{1,0:T(8,128)(2,1)} collective-permute-done((bf16[128,8192]{1,0:T(8,128)(2,1)}, bf16[128,8192]{1,0:T(8,128)(2,1)}, u32[]{:S(2)}, u32[]{:S(2)}) %collective-permute-start.3) | collective-permute-done | bytes 2097184 | tf_op jit(solution)/shard_map/ppermute | solution.py:159
  395.1 46.5 %collective-permute-done.2 = bf16[128,8192]{1,0:T(8,128)(2,1)} collective-permute-done((bf16[128,8192]{1,0:T(8,128)(2,1)}, bf16[128,8192]{1,0:T(8,128)(2,1)}, u32[]{:S(2)}, u32[]{:S(2)}) %collective-permute-start.2) | collective-permute-done | bytes 2097184 | tf_op jit(solution)/shard_map/ppermute | solution.py:159
  441.6 9.0 %add_bitcast_fusion = f32[1,128,8192]{2,1,0:T(8,128)} fusion(bf16[128,8192]{1,0:T(8,128)(2,1)} %collective-permute-done.4, bf16[128,8192]{1,0:T(8,128)(2,1)} %collective-permute-done.3, bf16[128,8192]{1,0:T(8,128)(2,1)} %collective-permute-done.2, f32[128]{0:T(128)S(1)} %broadcast_multiply_fusion, f32[128]{0:T(128)S(1)} %get-tuple-element.55, ...), kind=kLoop, calls=%fused_computation.44 | loop fusion | flops 14680064 | bytes 18908676 | tf_op jit(solution)/shard_map/broadcast_in_dim | solution.py:168
  (172 shorter events, 108.0 us)
Async XLA Ops:
  10.2 11.7 %all-to-all-start.2 = ((bf16[4,128,256]{1,2,0:T(8,128)(2,1)}), bf16[4,128,256]{1,2,0:T(8,128)(2,1)S(1)}, u32[]{:S(2)}, u32[]{:S(2)}) async-start(bf16[4,128,256]{1,2,0:T(8,128)(2,1)} %maximum_bitcast_fusion.13), calls=%async_computation.2 | async-start | bytes 524288 | tf_op jit(solution)/shard_map/all_to_all | solution.py:92
  21.9 10.9 %all-to-all-start = ((bf16[4,128,256]{1,2,0:T(8,128)(2,1)}), bf16[4,128,256]{1,2,0:T(8,128)(2,1)S(1)}, u32[]{:S(2)}, u32[]{:S(2)}) async-start(bf16[4,128,256]{1,2,0:T(8,128)(2,1)} %maximum_bitcast_fusion.12), calls=%async_computation | async-start | bytes 524288 | tf_op jit(solution)/shard_map/all_to_all | solution.py:92
  26.2 14.5 %copy-start.31 = (s32[1,2]{1,0:T(1,128)S(1)}, s32[1,2]{1,0:T(1,128)}, u32[]{:S(2)}) copy-start(s32[1,2]{1,0:T(1,128)} %param.22) | copy-start | bytes 28
  26.2 14.6 %copy-start.29 = (s32[3,16]{1,0:T(4,128)S(1)}, s32[3,16]{1,0:T(4,128)}, u32[]{:S(2)}) copy-start(s32[3,16]{1,0:T(4,128)} %param.23) | copy-start | bytes 580
  26.2 15.8 %copy-start.24 = (bf16[1,128,256]{2,1,0:T(8,128)(2,1)S(1)}, bf16[1,128,256]{2,1,0:T(8,128)(2,1)}, u32[]{:S(2)}) copy-start(bf16[1,128,256]{2,1,0:T(8,128)(2,1)} %param.13) | copy-start | bytes 196612
  34.2 31.0 %all-to-all-start.3 = ((bf16[8,512,256]{2,1,0:T(8,128)(2,1)}), bf16[8,512,256]{2,1,0:T(8,128)(2,1)S(1)}, u32[]{:S(2)}, u32[]{:S(2)}) async-start(bf16[8,512,256]{2,1,0:T(8,128)(2,1)} %stack.20), calls=%async_computation.3 | async-start | bytes 4194304 | tf_op jit(solution)/shard_map/all_to_all | solution.py:95
  40.7 32.8 %copy-start.11 = (bf16[1,128,2048]{1,2,0:T(8,128)(2,1)}, bf16[1,128,2048]{1,2,0:T(8,128)(2,1)S(1)}, u32[]{:S(2)}) copy-start(bf16[1,128,2048]{1,2,0:T(8,128)(2,1)S(1)} %copy.163) | copy-start | bytes 1572868
  42.0 56.9 %copy-start.22 = (bf16[128,128]{1,0:T(8,128)(2,1)}, bf16[128,128]{1,0:T(8,128)(2,1)S(1)}, u32[]{:S(2)}) copy-start(bf16[128,128]{1,0:T(8,128)(2,1)S(1)} %get-tuple-element.52) | copy-start | bytes 98308
  42.9 30.5 %copy-start.17 = (bf16[128,1,8,128]{0,3,2,1:T(8,128)(2,1)S(1)}, bf16[128,1,8,128]{0,3,2,1:T(8,128)(2,1)}, u32[]{:S(2)}) copy-start(bf16[128,1,8,128]{0,3,2,1:T(8,128)(2,1)} %get-tuple-element.44) | copy-start | bytes 786436
  66.8 29.5 %all-to-all-start.1 = ((bf16[8,512,256]{2,1,0:T(8,128)(2,1)}), bf16[8,512,256]{2,1,0:T(8,128)(2,1)}, u32[]{:S(2)}, u32[]{:S(2)}) async-start(bf16[8,512,256]{2,1,0:T(8,128)(2,1)} %stack.18), calls=%async_computation.1 | async-start | bytes 4194304 | tf_op jit(solution)/shard_map/all_to_all | solution.py:95
  71.3 126.5 %reduce-scatter.3.cloned.1.call-start = ((), (), s32[]{:S(2)}) async-start(), calls=%async_computation.7 | async-start | bytes 2359296 | tf_op jit(solution)/shard_map/reduce_scatter | solution.py:113
  144.8 107.2 %reduce-scatter.5.cloned.1.call-start = ((), (), s32[]{:S(2)}) async-start(), calls=%async_computation.8 | async-start | bytes 2359296 | tf_op jit(solution)/shard_map/reduce_scatter | solution.py:113
  158.6 14.5 %slice-start.5 = ((s8[17301504]{0:T(1024)(128)(4,1)}), s8[4194304]{0:T(1024)(128)(4,1)S(1)}, s32[]{:S(2)}) async-start(s8[17301504]{0:T(1024)(128)(4,1)} %bitcast.192), calls=%async_computation.14 | async-start | bytes 8388608
  158.6 14.5 %slice-start.6 = ((s8[17301504]{0:T(1024)(128)(4,1)}), s8[4194304]{0:T(1024)(128)(4,1)S(1)}, s32[]{:S(2)}) async-start(s8[17301504]{0:T(1024)(128)(4,1)} %bitcast.192), calls=%async_computation.15 | async-start | bytes 8388608
  158.6 14.5 %slice-start.7 = ((s8[17301504]{0:T(1024)(128)(4,1)}), s8[4194304]{0:T(1024)(128)(4,1)S(1)}, s32[]{:S(2)}) async-start(s8[17301504]{0:T(1024)(128)(4,1)} %bitcast.192), calls=%async_computation.16 | async-start | bytes 8388608
  158.7 14.5 %slice-start.8 = ((s8[17301504]{0:T(1024)(128)(4,1)}), s8[4194304]{0:T(1024)(128)(4,1)S(1)}, s32[]{:S(2)}) async-start(s8[17301504]{0:T(1024)(128)(4,1)} %bitcast.192), calls=%async_computation.17 | async-start | bytes 8388608
  268.8 8.2 %collective-permute-start = (bf16[2,128,8192]{2,1,0:T(8,128)(2,1)}, bf16[2,128,8192]{2,1,0:T(8,128)(2,1)}, u32[]{:S(2)}, u32[]{:S(2)}) collective-permute-start(bf16[2,128,8192]{2,1,0:T(8,128)(2,1)} %dynamic-slice_bitcast_fusion), channel_id=1, source_target_pairs={{0,1},{1,0},{2,3},{3,2},{4,5},{5,4},{6,7},{7,6},{8,9},{9,8},{10,11... | collective-permute-start | bytes 12582920 | tf_op jit(solution)/shard_map/ppermute | solution.py:141
  286.8 48.7 %collective-permute-start.1 = (bf16[128,8192]{1,0:T(8,128)(2,1)}, bf16[128,8192]{1,0:T(8,128)(2,1)}, u32[]{:S(2)}, u32[]{:S(2)}) collective-permute-start(bf16[128,8192]{1,0:T(8,128)(2,1)} %fusion.26), channel_id=1, source_target_pairs={{0,2},{1,3},{2,0},{3,1},{4,6},{5,7},{6,4},{7,5},{8,10},{9,11},{10,... | collective-permute-start | bytes 6291464 | tf_op jit(solution)/shard_map/ppermute | solution.py:146
  289.3 46.2 %copy-start.1 = (f32[2,128,8192]{2,1,0:T(8,128)S(1)}, f32[2,128,8192]{2,1,0:T(8,128)}, u32[]{:S(2)}) copy-start(f32[2,128,8192]{2,1,0:T(8,128)} %copy-done) | copy-start | bytes 25165828
  289.3 46.2 %copy-start.2 = (bf16[1,128,8192]{2,1,0:T(8,128)(2,1)S(1)}, bf16[1,128,8192]{2,1,0:T(8,128)(2,1)}, u32[]{:S(2)}) copy-start(bf16[1,128,8192]{2,1,0:T(8,128)(2,1)} %param.19) | copy-start | bytes 6291460
  343.2 26.3 %collective-permute-start.4 = (bf16[128,8192]{1,0:T(8,128)(2,1)}, bf16[128,8192]{1,0:T(8,128)(2,1)}, u32[]{:S(2)}, u32[]{:S(2)}) collective-permute-start(bf16[128,8192]{1,0:T(8,128)(2,1)} %fusion.58), channel_id=1, source_target_pairs={{96,0},{97,1},{98,2},{99,3},{100,4},{101,5},{102,6},{103,7},{104,8... | collective-permute-start | bytes 6291464 | tf_op jit(solution)/shard_map/ppermute | solution.py:159
  345.4 49.7 %collective-permute-start.3 = (bf16[128,8192]{1,0:T(8,128)(2,1)}, bf16[128,8192]{1,0:T(8,128)(2,1)}, u32[]{:S(2)}, u32[]{:S(2)}) collective-permute-start(bf16[128,8192]{1,0:T(8,128)(2,1)} %fusion.58), channel_id=1, source_target_pairs={{64,0},{96,32},{65,1},{97,33},{66,2},{98,34},{67,3},{99,35},{68,4}... | collective-permute-start | bytes 6291464 | tf_op jit(solution)/shard_map/ppermute | solution.py:159
  346.7 94.9 %collective-permute-start.2 = (bf16[128,8192]{1,0:T(8,128)(2,1)}, bf16[128,8192]{1,0:T(8,128)(2,1)}, u32[]{:S(2)}, u32[]{:S(2)}) collective-permute-start(bf16[128,8192]{1,0:T(8,128)(2,1)} %fusion.58), channel_id=1, source_target_pairs={{32,0},{64,32},{96,64},{33,1},{65,33},{97,65},{34,2},{66,34},{98,6... | collective-permute-start | bytes 6291464 | tf_op jit(solution)/shard_map/ppermute | solution.py:159
  352.6 14.8 %all-to-all-start.4 = ((bf16[4,128,512]{1,2,0:T(8,128)(2,1)}), bf16[4,128,512]{1,2,0:T(8,128)(2,1)S(1)}, u32[]{:S(2)}, u32[]{:S(2)}) async-start(bf16[4,128,512]{1,2,0:T(8,128)(2,1)} %copy_bitcast_fusion), calls=%async_computation.6 | async-start | bytes 1048576 | tf_op jit(solution)/shard_map/all_to_all | solution.py:120
  (34 other events, 216.6 us)
Sparse Core Ops, SparseCore 0:
  145.0 52.8 reduce-scatter.2
  200.2 51.8 reduce-scatter.4
